TPU v7x, 256 devices: a whole 4x4x8 slice. The times are simulated.
256 devices in a mesh: dp: 16 (over x, y_hi, core), seq: 16 (over z, y_lo).
Axes of the slice: x: 4, y: 4 (y_hi: 2, y_lo: 2; y = y_hi * 2 + y_lo), z: 8, core: 2. Of those that a mesh axis runs over, the one named last changes fastest.
Arguments:
- queries: bfloat16 [40960, 768], P(('dp', 'seq')), may hold values from -8 to 8
- keys: bfloat16 [40960, 768], P(('dp', 'seq')), may hold values from -8 to 8
- values: bfloat16 [40960, 768], P(('dp', 'seq')), may hold values from -6 to 6
- frames: bfloat16 [40960, 768], P(('dp', 'seq')), may hold values from -4 to 4
- upstream: bfloat16 [40960, 768], P(('dp', 'seq')), may hold values from -6 to 6
- lengths: int32 [16], P('dp'), may hold values from 640 to 2560, as said below
- conv_kernel: bfloat16 [32, 768], replicated, may hold values from -1 to 1
Outputs:
- out: bfloat16 [40960, 768], P(('dp', 'seq'))
- query_grad: bfloat16 [40960, 768], P(('dp', 'seq'))
- key_grad: bfloat16 [40960, 768], P(('dp', 'seq'))
- value_grad: bfloat16 [40960, 768], P(('dp', 'seq'))
- frame_grad: bfloat16 [40960, 768], P(('dp', 'seq'))
- kernel_grad: float32 [32, 768], replicated
Inputs may be any that keep to these rules, and one draw needn't show every extreme that they name: `lengths`: one utterance has all 2560 frames live and another has 640.
All inputs are finite; a program needn't handle non-finite values.
Results may differ from a plain program's by a relative error of at most 0.0262.
Values may be sent and summed in bfloat16 or wider, within the bound.
No kernel may reach another device: no remote copies, remote signals or barrier semaphores. Data moves between devices by JAX's collectives and lax.ppermute only.
A program may use at most 128 MiB of HBM per device.

v0:
```python
import jax
import jax.numpy as jnp
from jax import lax
from jax.sharding import Mesh
from jax.sharding import PartitionSpec as P

HEAD_DIM = 64
KERNEL = 32
GROUPS = 4


def shifted(x, axis, by):
    count = lax.axis_size(axis)
    pairs = [(i, i + by) for i in range(count) if 0 <= i + by < count]
    return lax.ppermute(x, axis, pairs)


def butterfly_sum(x, axes):
    for axis in axes:
        count = lax.axis_size(axis)
        step = 1
        while step < count:
            x = x + lax.ppermute(x, axis, [(i, i ^ step) for i in range(count)])
            step = step * 2
    return x


def per_device(queries, keys, values, frames, upstream, lengths, conv_kernel):
    rows = queries.shape[0]
    channels = queries.shape[1]
    sub_count = lax.axis_size("sb")
    block_count_a = lax.axis_size("sa")
    group = channels // sub_count
    head_count = group // HEAD_DIM
    row_count = rows * sub_count
    span = row_count * block_count_a
    block_index = lax.axis_index("sa")
    group_index = lax.axis_index("sb")
    first_row = block_index * row_count
    length = lengths[0]
    score_scale = HEAD_DIM ** (-0.5)
    stacked = jnp.stack([queries, keys, values, frames, upstream])
    mixed = lax.all_to_all(
        stacked.reshape(5, rows, sub_count, group), "sb", 2, 1, tiled=True
    ).reshape(5, row_count, group)
    queries_b = mixed[0]
    frames_b = mixed[3]
    upstream_b = mixed[4]
    kv_all = lax.all_gather(jnp.concatenate([mixed[1], mixed[2]], axis=1), "sa", axis=0, tiled=True)
    key_all = kv_all[:, :group]
    value_all = kv_all[:, group:]
    key_block = row_count
    block_count = span // key_block
    key_blocks = key_all.reshape(block_count, key_block, head_count, HEAD_DIM)
    value_blocks = value_all.reshape(block_count, key_block, head_count, HEAD_DIM)
    block_starts = jnp.arange(block_count, dtype=jnp.int32) * key_block
    query_heads = queries_b.reshape(row_count, head_count, HEAD_DIM)

    def block_scores(key_part, block_start):
        scores = (
            jnp.einsum("thd,khd->htk", query_heads, key_part, preferred_element_type=jnp.float32)
            * score_scale
        )
        key_live = block_start + jnp.arange(key_part.shape[0], dtype=jnp.int32) < length
        return jnp.where(key_live[None, None, :], scores, -jnp.inf)

    def running_total(state_pair, block_items):
        running_top, total_sum = state_pair
        key_part, block_start = block_items
        scores = block_scores(key_part, block_start)
        higher = jnp.maximum(running_top, jnp.max(scores, axis=2))
        total_sum = total_sum * jnp.exp(running_top - higher) + jnp.sum(
            jnp.exp(scores - higher[:, :, None]), axis=2
        )
        return ((higher, total_sum), None)

    start_state = (
        jnp.full((head_count, row_count), -1e30, jnp.float32),
        jnp.zeros((head_count, row_count), jnp.float32),
    )
    (running_top, total_sum), unused = lax.scan(
        running_total, start_state, (key_blocks, block_starts)
    )
    log_total = running_top + jnp.log(total_sum)

    def attend_block(attend_acc, block_items):
        key_part, value_part, block_start = block_items
        prob_bf = jnp.exp(block_scores(key_part, block_start) - log_total[:, :, None]).astype(
            jnp.bfloat16
        )
        return (
            attend_acc
            + jnp.einsum("htk,khd->thd", prob_bf, value_part, preferred_element_type=jnp.float32),
            None,
        )

    attend_acc, unused = lax.scan(
        attend_block,
        jnp.zeros((row_count, head_count, HEAD_DIM), jnp.float32),
        (key_blocks, value_blocks, block_starts),
    )
    attended = attend_acc.reshape(row_count, group).astype(jnp.bfloat16)
    frame_live = (first_row + jnp.arange(row_count, dtype=jnp.int32) < length)[:, None]
    hidden = (frames_b.astype(jnp.float32) + attended.astype(jnp.float32)).astype(jnp.bfloat16)
    masked = jnp.where(frame_live, hidden, jnp.zeros_like(hidden))
    past_rows = shifted(masked[row_count - (KERNEL - 1) :], "sa", 1)
    extended = jnp.concatenate([past_rows, masked], axis=0).astype(jnp.float32)
    weights = lax.dynamic_slice_in_dim(conv_kernel, group_index * group, group, axis=1).astype(
        jnp.float32
    )
    conv_out = jnp.zeros((row_count, group), jnp.float32)
    for tap_index in range(KERNEL):
        conv_out = (
            conv_out
            + weights[tap_index]
            * extended[KERNEL - 1 - tap_index : KERNEL - 1 - tap_index + row_count]
        )
    sig_conv = jax.nn.sigmoid(conv_out)
    out = (hidden.astype(jnp.float32) + conv_out * sig_conv).astype(jnp.bfloat16)
    loss_grad = jnp.where(frame_live, upstream_b.astype(jnp.float32), 0.0)
    conv_grad = (loss_grad * sig_conv * (1.0 + conv_out * (1.0 - sig_conv))).astype(jnp.bfloat16)
    conv_float = conv_grad.astype(jnp.float32)
    kernel_part = jnp.stack(
        [
            jnp.sum(
                conv_float * extended[KERNEL - 1 - tap_index : KERNEL - 1 - tap_index + row_count],
                axis=0,
            )
            for tap_index in range(KERNEL)
        ]
    )
    future_rows = shifted(conv_grad[: KERNEL - 1], "sa", -1)
    ahead_rows = jnp.concatenate([conv_grad, future_rows], axis=0).astype(jnp.float32)
    back_conv = jnp.zeros((row_count, group), jnp.float32)
    for tap_index in range(KERNEL):
        back_conv = back_conv + weights[tap_index] * ahead_rows[tap_index : tap_index + row_count]
    frame_grad = (loss_grad + jnp.where(frame_live, back_conv, 0.0)).astype(jnp.bfloat16)
    grad_heads = frame_grad.reshape(row_count, head_count, HEAD_DIM)
    attended_heads = attended.reshape(row_count, head_count, HEAD_DIM)
    delta_rows = jnp.sum(
        grad_heads.astype(jnp.float32) * attended_heads.astype(jnp.float32), axis=2
    ).T

    def score_grads(key_part, value_part, block_start):
        soft_weights = jnp.exp(block_scores(key_part, block_start) - log_total[:, :, None])
        prob_grad = jnp.einsum(
            "thd,khd->htk", grad_heads, value_part, preferred_element_type=jnp.float32
        )
        score_grad = (soft_weights * (prob_grad - delta_rows[:, :, None])).astype(jnp.bfloat16)
        return (soft_weights.astype(jnp.bfloat16), score_grad)

    def gradient_block(query_acc, block_items):
        key_part, value_part, block_start = block_items
        prob_bf, score_grad = score_grads(key_part, value_part, block_start)
        query_acc = query_acc + jnp.einsum(
            "htk,khd->thd", score_grad, key_part, preferred_element_type=jnp.float32
        )
        key_term = (
            jnp.einsum("htk,thd->khd", score_grad, query_heads, preferred_element_type=jnp.float32)
            * score_scale
        )
        value_term = jnp.einsum(
            "htk,thd->khd", prob_bf, grad_heads, preferred_element_type=jnp.float32
        )
        grad_terms = jnp.concatenate(
            [key_term.reshape(key_block, group), value_term.reshape(key_block, group)], axis=1
        )
        return (query_acc, grad_terms)

    query_acc, grad_terms = lax.scan(
        gradient_block,
        jnp.zeros((row_count, head_count, HEAD_DIM), jnp.float32),
        (key_blocks, value_blocks, block_starts),
    )
    own_rows = lax.psum_scatter(
        grad_terms.reshape(span, 2 * group).astype(jnp.bfloat16),
        "sa",
        scatter_dimension=0,
        tiled=True,
    ).astype(jnp.float32)
    key_grad = own_rows[:, :group].astype(jnp.bfloat16)
    value_grad = own_rows[:, group:].astype(jnp.bfloat16)
    query_grad = (query_acc * score_scale).reshape(row_count, group).astype(jnp.bfloat16)
    kernel_full = lax.dynamic_update_slice_in_dim(
        jnp.zeros((KERNEL, channels), jnp.float32), kernel_part, group_index * group, axis=1
    )
    kernel_total = butterfly_sum(kernel_full, ("sb", "sa", "dp"))
    kernel_grad = kernel_total / lax.axis_size("dp")
    results = jnp.stack([out, query_grad, key_grad, value_grad, frame_grad])
    spread = lax.all_to_all(
        results.reshape(5, sub_count, rows, 1, group), "sb", 1, 3, tiled=True
    ).reshape(5, rows, channels)
    return (spread[0], spread[1], spread[2], spread[3], spread[4], kernel_grad)


def solution(mesh):
    seq_count = mesh.shape["seq"]
    split_mesh = Mesh(
        mesh.devices.reshape(mesh.shape["dp"], seq_count // GROUPS, GROUPS), ("dp", "sa", "sb")
    )
    rows_spec = P(("dp", "sa", "sb"), None)
    placed = (rows_spec, rows_spec, rows_spec, rows_spec, rows_spec, P("dp"), P())
    return jax.shard_map(
        per_device,
        mesh=split_mesh,
        in_specs=placed,
        out_specs=(rows_spec, rows_spec, rows_spec, rows_spec, rows_spec, P()),
        check_vma=False,
    )
```

profile of v0, /device:TPU:2, one launch (start us, length us, event | category | flops | bytes accessed | tf_op | source)
XLA Modules:
  0.0 392.6 jit_solution(232273346341479808)
XLA Ops:
  12.7 24.6 %all_to_all.30 = bf16[5,160,4,192]{3,1,0,2:T(8,128)(2,1)S(1)} all-to-all(bf16[5,160,4,192]{3,1,0,2:T(8,128)(2,1)S(1)} %copy.80), channel_id=1, replica_groups=mesh['dp'=16,'sa'=4,'sb'=4] {'sb'}, dimensions={2} | all-to-all | bytes 2457600 | tf_op jit(solution)/shard_map/all_to_all | solution.py:43
  41.8 47.3 %all-gather.2.cloned.1.call-done = bf16[2560,384]{1,0:T(8,128)(2,1)} async-done(((bf16[640,384]{1,0:T(8,128)(2,1)}), bf16[2560,384]{1,0:T(8,128)(2,1)}) %all-gather.2.cloned.1.call-update) | async-done | bytes 1966096 | tf_op jit(solution)/shard_map/all_gather | solution.py:49
  95.8 40.8 %while.37 = (s32[]{:T(128)}, f32[3,640]{1,0:T(4,128)S(1)}, f32[3,640]{1,0:T(4,128)S(1)}, s32[4]{0:T(128)}, s32[]{:T(128)}, /*index=5*/bf16[4,640,3,64]{1,3,2,0:T...) while((s32[]{:T(128)}, f32[3,640]{1,0:T(4,128)S(1)}, f32[3,640]{1,0:T(4,128)S(1)}, ...), condition=%wide.region_3.4_spmd.clone, body=%wide.region_0.3_spmd.clone.sunk | while | flops 165898880 | bytes 10424316 | solution.py:81
  98.4 4.1 %bitcast_reduce_fusion.2 = (f32[3,640]{1,0:T(4,128)S(1)}, f32[3,640,640]{2,1,0:T(8,128)}) fusion(pred[640]{0:T(1024)(128)(4,1)S(1)} %add_compare_fusion.7, bf16[640,3,64]{0,2,1:T(8,128)(2,1)S(1)} %get-tuple-element.670, bf16[4,640,3,64]{1,3,2,0:T(8,128)(2,1)} %get-tuple-element.669, s32[]{:T(128)} %get-tuple-element.655), kind=kOutput, calls=%fused_computation.1.clone.1 | convolution fusion | flops 160970880 | bytes 5415552 | tf_op jit(solution)/shard_map/while/body/eval_jaxpr/thd,khd->htk/dot_general | solution.py:61
  102.5 3.4 fusion.146
  108.6 4.1 %bitcast_reduce_fusion.2 = (f32[3,640]{1,0:T(4,128)S(1)}, f32[3,640,640]{2,1,0:T(8,128)}) fusion(pred[640]{0:T(1024)(128)(4,1)S(1)} %add_compare_fusion.7, bf16[640,3,64]{0,2,1:T(8,128)(2,1)S(1)} %get-tuple-element.670, bf16[4,640,3,64]{1,3,2,0:T(8,128)(2,1)} %get-tuple-element.669, s32[]{:T(128)} %get-tuple-element.655), kind=kOutput, calls=%fused_computation.1.clone.1 | convolution fusion | flops 160970880 | bytes 5415552 | tf_op jit(solution)/shard_map/while/body/eval_jaxpr/thd,khd->htk/dot_general | solution.py:61
  112.7 3.4 fusion.146
  118.8 4.1 %bitcast_reduce_fusion.2 = (f32[3,640]{1,0:T(4,128)S(1)}, f32[3,640,640]{2,1,0:T(8,128)}) fusion(pred[640]{0:T(1024)(128)(4,1)S(1)} %add_compare_fusion.7, bf16[640,3,64]{0,2,1:T(8,128)(2,1)S(1)} %get-tuple-element.670, bf16[4,640,3,64]{1,3,2,0:T(8,128)(2,1)} %get-tuple-element.669, s32[]{:T(128)} %get-tuple-element.655), kind=kOutput, calls=%fused_computation.1.clone.1 | convolution fusion | flops 160970880 | bytes 5415552 | tf_op jit(solution)/shard_map/while/body/eval_jaxpr/thd,khd->htk/dot_general | solution.py:61
  123.0 3.4 fusion.146
  129.0 4.1 %bitcast_reduce_fusion.2 = (f32[3,640]{1,0:T(4,128)S(1)}, f32[3,640,640]{2,1,0:T(8,128)}) fusion(pred[640]{0:T(1024)(128)(4,1)S(1)} %add_compare_fusion.7, bf16[640,3,64]{0,2,1:T(8,128)(2,1)S(1)} %get-tuple-element.670, bf16[4,640,3,64]{1,3,2,0:T(8,128)(2,1)} %get-tuple-element.669, s32[]{:T(128)} %get-tuple-element.655), kind=kOutput, calls=%fused_computation.1.clone.1 | convolution fusion | flops 160970880 | bytes 5415552 | tf_op jit(solution)/shard_map/while/body/eval_jaxpr/thd,khd->htk/dot_general | solution.py:61
  133.2 3.4 fusion.146
  138.2 24.5 %while.38 = (s32[]{:T(128)}, f32[640,3,64]{0,2,1:T(8,128)}, bf16[4,640,3,64]{1,3,2,0:T(8,128)(2,1)S(1)}, s32[4]{0:T(128)}, s32[]{:T(128)}, /*index=5*/bf16[4,640...) while((s32[]{:T(128)}, f32[640,3,64]{0,2,1:T(8,128)}, ...), condition=%wide.region_5.6_spmd.clone, body=%wide.region_4.5_spmd.clone.sunk | while | flops 319735040 | bytes 1733379 | solution.py:97
  140.8 3.4 fusion.151
  146.8 3.6 fusion.151
  152.9 3.6 fusion.151
  159.1 3.6 fusion.151
  165.3 5.2 %collective-permute-start = (bf16[31,192]{1,0:T(8,128)(2,1)S(1)}, bf16[31,192]{1,0:T(8,128)(2,1)S(1)}, u32[]{:S(2)}, u32[]{:S(2)}) collective-permute-start(bf16[31,192]{1,0:T(8,128)(2,1)S(1)} %slice.531), channel_id=1, source_target_pairs={{0,4},{4,8},{8,12},{1,5},{5,9},{9,13},{2,6},{6,10},{10,14},{3,7},{... | collective-permute-start | bytes 35720 | tf_op jit(solution)/shard_map/ppermute | solution.py:15
  172.1 7.1 %fusion.71 = (f32[192]{0:T(256)}, f32[192]{0:T(256)}, f32[192]{0:T(256)}, f32[192]{0:T(256)}, f32[192]{0:T(256)}, /*index=5*/f32[192]{0:T(256)}, f32[192]{0:T(25...) fusion(f32[671,192]{1,0:T(8,128)S(1)} %maximum_convert_fusion, ...), kind=kLoop, calls=%fused_computation.113 | loop fusion | flops 13636224 | bytes 16750720 | tf_op jit(solution)/shard_map/reduce_sum | solution.py:125
  180.5 5.6 %collective-permute-done.1 = bf16[31,192]{1,0:T(8,128)(2,1)S(1)} collective-permute-done((bf16[31,192]{1,0:T(8,128)(2,1)S(1)}, bf16[31,192]{1,0:T(8,128)(2,1)S(1)}, u32[]{:S(2)}, u32[]{:S(2)}) %collective-permute-start.1) | collective-permute-done | bytes 11936 | tf_op jit(solution)/shard_map/ppermute | solution.py:15
  186.2 3.1 fusion.75
  191.2 70.0 %while.39 = (s32[]{:T(128)}, f32[640,3,64]{0,2,1:T(8,128)}, bf16[4,640,384]{2,1,0:T(8,128)(2,1)}, bf16[4,640,3,64]{1,3,2,0:T(8,128)(2,1)}, s32[4]{0:T(128)}, /*i...) while((s32[]{:T(128)}, f32[640,3,64]{0,2,1:T(8,128)}, ...), condition=%wide.region_8.9_spmd.clone, body=%wide.region_7.8_spmd.clone.sunk | while | flops 800195840 | bytes 28292124 | solution.py:170
  261.2 2.9 fusion.70
  264.8 44.9 %reduce-scatter.2.cloned.1.call-done = bf16[640,384]{1,0:T(8,128)(2,1)} async-done(((bf16[2560,384]{1,0:T(8,128)(2,1)}), bf16[640,384]{1,0:T(8,128)(2,1)}) %reduce-scatter.2.cloned.1.call-update) | async-done | bytes 491536 | tf_op jit(solution)/shard_map/reduce_scatter | solution.py:175
  312.4 3.6 all-to-all-start.1
  319.2 19.0 %collective-permute-done.2 = f32[32,768]{1,0:T(8,128)S(1)} collective-permute-done((f32[32,768]{1,0:T(8,128)S(1)}, f32[32,768]{1,0:T(8,128)S(1)}, u32[]{:S(2)}, u32[]{:S(2)}) %collective-permute-start.2) | collective-permute-done | bytes 98336 | tf_op jit(solution)/shard_map/ppermute | solution.py:23
  340.2 3.2 collective-permute-done.3
  345.9 4.4 %collective-permute-done.4 = f32[32,768]{1,0:T(8,128)S(1)} collective-permute-done((f32[32,768]{1,0:T(8,128)S(1)}, f32[32,768]{1,0:T(8,128)S(1)}, u32[]{:S(2)}, u32[]{:S(2)}) %collective-permute-start.4) | collective-permute-done | bytes 98336 | tf_op jit(solution)/shard_map/ppermute | solution.py:23
  352.8 7.1 %collective-permute-done.5 = f32[32,768]{1,0:T(8,128)S(1)} collective-permute-done((f32[32,768]{1,0:T(8,128)S(1)}, f32[32,768]{1,0:T(8,128)S(1)}, u32[]{:S(2)}, u32[]{:S(2)}) %collective-permute-start.5) | collective-permute-done | bytes 98336 | tf_op jit(solution)/shard_map/ppermute | solution.py:23
  361.3 3.2 collective-permute-start.7
  364.5 3.3 collective-permute-done.7
  368.3 4.2 %collective-permute-done.8 = f32[32,768]{1,0:T(8,128)S(1)} collective-permute-done((f32[32,768]{1,0:T(8,128)S(1)}, f32[32,768]{1,0:T(8,128)S(1)}, u32[]{:S(2)}, u32[]{:S(2)}) %collective-permute-start.8) | collective-permute-done | bytes 98336 | tf_op jit(solution)/shard_map/ppermute | solution.py:23
  374.7 4.0 %collective-permute-done.9 = f32[32,768]{1,0:T(8,128)S(1)} collective-permute-done((f32[32,768]{1,0:T(8,128)S(1)}, f32[32,768]{1,0:T(8,128)S(1)}, u32[]{:S(2)}, u32[]{:S(2)}) %collective-permute-start.9) | collective-permute-done | bytes 98336 | tf_op jit(solution)/shard_map/ppermute | solution.py:23
  (252 shorter events, 139.3 us)
Async XLA Ops:
  7.2 81.9 %all-gather.2.cloned.1.call-start = ((), (), s32[]{:S(2)}) async-start(), calls=%async_computation.3 | async-start | bytes 2457600 | tf_op jit(solution)/shard_map/all_gather | solution.py:49
  37.4 127.7 %copy-start.3 = (bf16[1,4,160,1,192]{4,2,0,1,3:T(8,128)(2,1)}, bf16[1,4,160,1,192]{4,2,0,1,3:T(8,128)(2,1)S(1)}, u32[]{:S(2)}) copy-start(bf16[1,4,160,1,192]{4,2,0,1,3:T(8,128)(2,1)S(1)} %get-tuple-element.447) | copy-start | bytes 737284
  38.5 271.2 %reduce-scatter.2.cloned.1.call-start = ((), (), s32[]{:S(2)}) async-start(), calls=%async_computation.4 | async-start | bytes 2457600 | tf_op jit(solution)/shard_map/reduce_scatter | solution.py:175
  163.7 8.3 %copy-start.13 = (f32[1,192]{1,0:T(1,128)S(1)}, f32[1,192]{1,0:T(1,128)}, u32[]{:S(2)}) copy-start(f32[1,192]{1,0:T(1,128)} %get-tuple-element.453) | copy-start | bytes 2308
  163.7 8.3 %copy-start.14 = (f32[1,192]{1,0:T(1,128)S(1)}, f32[1,192]{1,0:T(1,128)}, u32[]{:S(2)}) copy-start(f32[1,192]{1,0:T(1,128)} %get-tuple-element.454) | copy-start | bytes 2308
  163.7 8.3 %copy-start.15 = (f32[1,192]{1,0:T(1,128)S(1)}, f32[1,192]{1,0:T(1,128)}, u32[]{:S(2)}) copy-start(f32[1,192]{1,0:T(1,128)} %get-tuple-element.455) | copy-start | bytes 2308
  163.7 8.3 %copy-start.16 = (f32[1,192]{1,0:T(1,128)S(1)}, f32[1,192]{1,0:T(1,128)}, u32[]{:S(2)}) copy-start(f32[1,192]{1,0:T(1,128)} %get-tuple-element.456) | copy-start | bytes 2308
  163.7 8.3 %copy-start.17 = (f32[1,192]{1,0:T(1,128)S(1)}, f32[1,192]{1,0:T(1,128)}, u32[]{:S(2)}) copy-start(f32[1,192]{1,0:T(1,128)} %get-tuple-element.457) | copy-start | bytes 2308
  163.7 8.3 %copy-start.18 = (f32[1,192]{1,0:T(1,128)S(1)}, f32[1,192]{1,0:T(1,128)}, u32[]{:S(2)}) copy-start(f32[1,192]{1,0:T(1,128)} %get-tuple-element.458) | copy-start | bytes 2308
  163.7 8.3 %copy-start.19 = (f32[1,192]{1,0:T(1,128)S(1)}, f32[1,192]{1,0:T(1,128)}, u32[]{:S(2)}) copy-start(f32[1,192]{1,0:T(1,128)} %get-tuple-element.459) | copy-start | bytes 2308
  163.7 8.3 %copy-start.20 = (f32[1,192]{1,0:T(1,128)S(1)}, f32[1,192]{1,0:T(1,128)}, u32[]{:S(2)}) copy-start(f32[1,192]{1,0:T(1,128)} %get-tuple-element.460) | copy-start | bytes 2308
  163.7 8.3 %copy-start.21 = (f32[1,192]{1,0:T(1,128)S(1)}, f32[1,192]{1,0:T(1,128)}, u32[]{:S(2)}) copy-start(f32[1,192]{1,0:T(1,128)} %get-tuple-element.461) | copy-start | bytes 2308
  163.8 8.3 %copy-start.22 = (f32[1,192]{1,0:T(1,128)S(1)}, f32[1,192]{1,0:T(1,128)}, u32[]{:S(2)}) copy-start(f32[1,192]{1,0:T(1,128)} %get-tuple-element.462) | copy-start | bytes 2308
  163.8 8.3 %copy-start.23 = (f32[1,192]{1,0:T(1,128)S(1)}, f32[1,192]{1,0:T(1,128)}, u32[]{:S(2)}) copy-start(f32[1,192]{1,0:T(1,128)} %get-tuple-element.463) | copy-start | bytes 2308
  163.8 8.3 %copy-start.24 = (f32[1,192]{1,0:T(1,128)S(1)}, f32[1,192]{1,0:T(1,128)}, u32[]{:S(2)}) copy-start(f32[1,192]{1,0:T(1,128)} %get-tuple-element.464) | copy-start | bytes 2308
  163.8 8.3 %copy-start.25 = (f32[1,192]{1,0:T(1,128)S(1)}, f32[1,192]{1,0:T(1,128)}, u32[]{:S(2)}) copy-start(f32[1,192]{1,0:T(1,128)} %get-tuple-element.465) | copy-start | bytes 2308
  163.8 8.3 %copy-start.26 = (f32[1,192]{1,0:T(1,128)S(1)}, f32[1,192]{1,0:T(1,128)}, u32[]{:S(2)}) copy-start(f32[1,192]{1,0:T(1,128)} %get-tuple-element.466) | copy-start | bytes 2308
  163.8 8.3 %copy-start.27 = (f32[1,192]{1,0:T(1,128)S(1)}, f32[1,192]{1,0:T(1,128)}, u32[]{:S(2)}) copy-start(f32[1,192]{1,0:T(1,128)} %get-tuple-element.467) | copy-start | bytes 2308
  163.8 8.3 %copy-start.28 = (f32[1,192]{1,0:T(1,128)S(1)}, f32[1,192]{1,0:T(1,128)}, u32[]{:S(2)}) copy-start(f32[1,192]{1,0:T(1,128)} %get-tuple-element.468) | copy-start | bytes 2308
  165.3 6.5 %collective-permute-start = (bf16[31,192]{1,0:T(8,128)(2,1)S(1)}, bf16[31,192]{1,0:T(8,128)(2,1)S(1)}, u32[]{:S(2)}, u32[]{:S(2)}) collective-permute-start(bf16[31,192]{1,0:T(8,128)(2,1)S(1)} %slice.531), channel_id=1, source_target_pairs={{0,4},{4,8},{8,12},{1,5},{5,9},{9,13},{2,6},{6,10},{10,14},{3,7},{... | collective-permute-start | bytes 35720 | tf_op jit(solution)/shard_map/ppermute | solution.py:15
  179.2 10.2 %copy-start.2 = (bf16[640,192]{1,0:T(8,128)(2,1)}, bf16[640,192]{1,0:T(8,128)(2,1)S(1)}, u32[]{:S(2)}) copy-start(bf16[640,192]{1,0:T(8,128)(2,1)S(1)} %get-tuple-element.432) | copy-start | bytes 737284
  179.2 6.9 %collective-permute-start.1 = (bf16[31,192]{1,0:T(8,128)(2,1)S(1)}, bf16[31,192]{1,0:T(8,128)(2,1)S(1)}, u32[]{:S(2)}, u32[]{:S(2)}) collective-permute-start(bf16[31,192]{1,0:T(8,128)(2,1)S(1)} %slice.596), channel_id=1, source_target_pairs={{4,0},{8,4},{12,8},{5,1},{9,5},{13,9},{6,2},{10,6},{14,10},{7,3},{... | collective-permute-start | bytes 35720 | tf_op jit(solution)/shard_map/ppermute | solution.py:15
  264.2 46.8 %copy-start.5 = (bf16[640,192]{1,0:T(8,128)(2,1)S(1)}, bf16[640,192]{1,0:T(8,128)(2,1)}, u32[]{:S(2)}) copy-start(bf16[640,192]{1,0:T(8,128)(2,1)} %copy-done.4) | copy-start | bytes 737284
  312.4 66.9 %all-to-all-start.1 = ((bf16[5,4,160,1,192]{4,2,3,0,1:T(8,128)(2,1)}), bf16[5,4,160,1,192]{4,2,3,0,1:T(8,128)(2,1)S(1)}, u32[]{:S(2)}, u32[]{:S(2)}) async-start(bf16[5,4,160,1,192]{4,2,3,0,1:T(8,128)(2,1)} %copy.93), calls=%async_computation.2 | async-start | bytes 3276800 | tf_op jit(solution)/shard_map/all_to_all | solution.py:190
  316.8 21.4 %collective-permute-start.2 = (f32[32,768]{1,0:T(8,128)S(1)}, f32[32,768]{1,0:T(8,128)S(1)}, u32[]{:S(2)}, u32[]{:S(2)}) collective-permute-start(f32[32,768]{1,0:T(8,128)S(1)} %dynamic_update_slice.9), channel_id=1, source_target_pairs={{0,1},{1,0},{2,3},{3,2},{4,5},{5,4},{6,7},{7,6},{8,9},{9,8},{10,11... | collective-permute-start | bytes 294920 | tf_op jit(solution)/shard_map/ppermute | solution.py:23
  338.7 4.7 %collective-permute-start.3 = (f32[32,768]{1,0:T(8,128)S(1)}, f32[32,768]{1,0:T(8,128)S(1)}, u32[]{:S(2)}, u32[]{:S(2)}) collective-permute-start(f32[32,768]{1,0:T(8,128)S(1)} %add.364), channel_id=1, source_target_pairs={{0,2},{1,3},{2,0},{3,1},{4,6},{5,7},{6,4},{7,5},{8,10},{9,11},{10,... | collective-permute-start | bytes 294920 | tf_op jit(solution)/shard_map/ppermute | solution.py:23
  343.5 6.8 %collective-permute-start.4 = (f32[32,768]{1,0:T(8,128)S(1)}, f32[32,768]{1,0:T(8,128)S(1)}, u32[]{:S(2)}, u32[]{:S(2)}) collective-permute-start(f32[32,768]{1,0:T(8,128)S(1)} %add.365), channel_id=1, source_target_pairs={{0,4},{4,0},{8,12},{12,8},{1,5},{5,1},{9,13},{13,9},{2,6},{6,2},{1... | collective-permute-start | bytes 294920 | tf_op jit(solution)/shard_map/ppermute | solution.py:23
  350.3 9.6 %collective-permute-start.5 = (f32[32,768]{1,0:T(8,128)S(1)}, f32[32,768]{1,0:T(8,128)S(1)}, u32[]{:S(2)}, u32[]{:S(2)}) collective-permute-start(f32[32,768]{1,0:T(8,128)S(1)} %add.366), channel_id=1, source_target_pairs={{0,8},{4,12},{8,0},{12,4},{1,9},{5,13},{9,1},{13,5},{2,10},{6,14},... | collective-permute-start | bytes 294920 | tf_op jit(solution)/shard_map/ppermute | solution.py:23
  359.9 1.4 collective-permute-start.6
  361.3 6.4 %collective-permute-start.7 = (f32[32,768]{1,0:T(8,128)S(1)}, f32[32,768]{1,0:T(8,128)S(1)}, u32[]{:S(2)}, u32[]{:S(2)}) collective-permute-start(f32[32,768]{1,0:T(8,128)S(1)} %add.368), channel_id=1, source_target_pairs={{0,32},{16,48},{32,0},{48,16},{64,96},{80,112},{96,64},{112,80},{1... | collective-permute-start | bytes 294920 | tf_op jit(solution)/shard_map/ppermute | solution.py:23
  367.8 4.7 %collective-permute-start.8 = (f32[32,768]{1,0:T(8,128)S(1)}, f32[32,768]{1,0:T(8,128)S(1)}, u32[]{:S(2)}, u32[]{:S(2)}) collective-permute-start(f32[32,768]{1,0:T(8,128)S(1)} %add.369), channel_id=1, source_target_pairs={{0,64},{16,80},{32,96},{48,112},{64,0},{80,16},{96,32},{112,48},{1... | collective-permute-start | bytes 294920 | tf_op jit(solution)/shard_map/ppermute | solution.py:23
  372.5 6.2 %collective-permute-start.9 = (f32[32,768]{1,0:T(8,128)S(1)}, f32[32,768]{1,0:T(8,128)S(1)}, u32[]{:S(2)}, u32[]{:S(2)}) collective-permute-start(f32[32,768]{1,0:T(8,128)S(1)} %add.370), channel_id=1, source_target_pairs={{0,128},{16,144},{32,160},{48,176},{64,192},{80,208},{96,224},{112... | collective-permute-start | bytes 294920 | tf_op jit(solution)/shard_map/ppermute | solution.py:23
  (28 other events, 110.1 us)
Sparse Core Ops, SparseCore 0:
  38.6 50.4 all-gather.1
  261.3 48.2 reduce-scatter.1
where the time goes:
time: 395 us; the launch traced here: 393 us
  waiting for transfers between devices  145 us (37%)
  matrix products  71.1 us (18%)
  local copies, waits for them, and re-layouts  59.1 us (15%)
  other arithmetic  52.1 us (13%)
  starting transfers between devices  25 us (6%)
  blocking collectives  24.6 us (6%)
  between operations  15.7 us (4%)
    all_gather x1, waiting for transfers between devices, per_device(): lax.all_gather(jnp.concatenate([mixed[1], mixed[2]], axis=1), 'sa', axis=...  47.3 us
    ppermute x8, waiting for transfers between devices, butterfly_sum(): x = x + lax.ppermute(x, axis, [(i, i ^ step) for i in range(count)])  46.5 us
    reduce_scatter x1, waiting for transfers between devices, per_device(): lax.psum_scatter(grad_terms.reshape(span, 2 * group).astype(jnp.bfloat16)...  44.9 us
    all_to_all x1, blocking collectives, per_device(): lax.all_to_all(stacked.reshape(5, rows, sub_count, group), 'sb', 2, 1, ti...  24.6 us
    dot_general x8, matrix products, block_scores(): jnp.einsum('thd,khd->htk', query_heads, key_part, preferred_element_type=...  23.7 us
    lt x12, other arithmetic, block_scores(): block_start + jnp.arange(key_part.shape[0], dtype=jnp.int32) < length  15.6 us
    dynamic_slice x12, local copies, waits for them, and re-layouts, per_device(): lax.scan(running_total, start_state, (key_blocks, block_starts))  15.6 us
    dynamic_update_slice x8, local copies, waits for them, and re-layouts, per_device(): lax.scan(gradient_block, jnp.zeros((row_count, head_count, HEAD_DIM), jnp...  15.5 us
  transfers between devices with their start and end apart: 13, of which 12 were waited for; matrix products, arithmetic and copies ran while one was open for 2% of the time, Pallas kernels for 0%

commit v1 on v0

--- a/solution.py
+++ b/solution.py
@@ -3,10 +3,24 @@
 from jax import lax
 from jax.sharding import Mesh
 from jax.sharding import PartitionSpec as P
+from jax.lax import all_to_all, axis_size
 
 HEAD_DIM = 64
 KERNEL = 32
 GROUPS = 4
+
+
+def lead_the_racks(x0):
+    everything = jnp.concatenate(
+        all_to_all(
+            jnp.stack([x0 for _ in range(axis_size("sa"))]),
+            split_axis=0,
+            concat_axis=0,
+            axis_name="sa",
+        ),
+        0,
+    )
+    return everything
 
 
 def shifted(x, axis, by):
@@ -46,7 +60,7 @@
     queries_b = mixed[0]
     frames_b = mixed[3]
     upstream_b = mixed[4]
-    kv_all = lax.all_gather(jnp.concatenate([mixed[1], mixed[2]], axis=1), "sa", axis=0, tiled=True)
+    kv_all = lead_the_racks(jnp.concatenate([mixed[1], mixed[2]], axis=1))
     key_all = kv_all[:, :group]
     value_all = kv_all[:, group:]
     key_block = row_count

time: 395 us -> 394 us (level)
  starting transfers between devices: 25 us -> 41.2 us
  waiting for transfers between devices: 145 us -> 130 us
    all_gather x1 -> x0, waiting for transfers between devices: 47.3 us -> none  [per_device(): lax.all_gather(jnp.concatenate([mixed[1], mixed[2]], axis=1), 'sa', axis=...]
    all_to_all x0 -> x1, waiting for transfers between devices: none -> 32.5 us  [lead_the_racks(): all_to_all(jnp.stack([x0 for _ in range(axis_size('sa'))]), split_axis=0,...]
    ppermute x2, starting transfers between devices: 6.53 us -> 15.4 us  [shifted(): return lax.ppermute(x, axis, pairs)]
    all_to_all x0 -> x1, starting transfers between devices: none -> 7.56 us  [lead_the_racks(): all_to_all(jnp.stack([x0 for _ in range(axis_size('sa'))]), split_axis=0,...]
where the time goes in v1:
time: 394 us; the launch traced here: 392 us
  waiting for transfers between devices  130 us (33%)
  matrix products  68 us (17%)
  local copies, waits for them, and re-layouts  62.6 us (16%)
  other arithmetic  50 us (13%)
  starting transfers between devices  41.2 us (10%)
  blocking collectives  24.6 us (6%)
  between operations  15.7 us (4%)
    ppermute x8, waiting for transfers between devices, butterfly_sum(): x = x + lax.ppermute(x, axis, [(i, i ^ step) for i in range(count)])  46.8 us
    reduce_scatter x1, waiting for transfers between devices, per_device(): lax.psum_scatter(grad_terms.reshape(span, 2 * group).astype(jnp.bfloat16)...  44.8 us
    all_to_all x1, waiting for transfers between devices, lead_the_racks(): all_to_all(jnp.stack([x0 for _ in range(axis_size('sa'))]), split_axis=0,...  32.5 us
    all_to_all x1, blocking collectives, per_device(): lax.all_to_all(stacked.reshape(5, rows, sub_count, group), 'sb', 2, 1, ti...  24.6 us
    dot_general x8, matrix products, block_scores(): jnp.einsum('thd,khd->htk', query_heads, key_part, preferred_element_type=...  23.7 us
    lt x12, other arithmetic, block_scores(): block_start + jnp.arange(key_part.shape[0], dtype=jnp.int32) < length  15.9 us
    dynamic_slice x12, local copies, waits for them, and re-layouts, per_device(): lax.scan(running_total, start_state, (key_blocks, block_starts))  15.8 us
    dynamic_update_slice x8, local copies, waits for them, and re-layouts, per_device(): lax.scan(gradient_block, jnp.zeros((row_count, head_count, HEAD_DIM), jnp...  15.5 us
  transfers between devices with their start and end apart: 13, of which 12 were waited for; matrix products, arithmetic and copies ran while one was open for 2% of the time, Pallas kernels for 0%

profile of v1, /device:TPU:2, one launch (start us, length us, event | category | flops | bytes accessed | tf_op | source)
XLA Modules:
  0.0 392.2 jit_solution(11468851117789124872)
XLA Ops:
  12.6 24.6 %all_to_all.35 = bf16[5,160,4,192]{3,1,0,2:T(8,128)(2,1)S(1)} all-to-all(bf16[5,160,4,192]{3,1,0,2:T(8,128)(2,1)S(1)} %copy.78), channel_id=1, replica_groups=mesh['dp'=16,'sa'=4,'sb'=4] {'sb'}, dimensions={2} | all-to-all | bytes 2457600 | tf_op jit(solution)/shard_map/all_to_all | solution.py:57
  40.1 7.6 %all-to-all-start.1 = ((bf16[4,640,384]{1,2,0:T(8,128)(2,1)}), bf16[4,640,384]{1,2,0:T(8,128)(2,1)}, u32[]{:S(2)}, u32[]{:S(2)}) async-start(bf16[4,640,384]{1,2,0:T(8,128)(2,1)} %stack.146), calls=%async_computation.1 | async-start | bytes 3932160 | tf_op jit(solution)/shard_map/all_to_all | solution.py:15
  50.9 32.5 %all-to-all-done.1 = bf16[4,640,384]{1,2,0:T(8,128)(2,1)} async-done(((bf16[4,640,384]{1,2,0:T(8,128)(2,1)}), bf16[4,640,384]{1,2,0:T(8,128)(2,1)}, u32[]{:S(2)}, u32[]{:S(2)}) %all-to-all-start.1) | async-done | bytes 1966112 | tf_op jit(solution)/shard_map/all_to_all | solution.py:15
  83.3 2.8 copy.80
  90.7 41.1 %while.37 = (s32[]{:T(128)}, f32[3,640]{1,0:T(4,128)S(1)}, f32[3,640]{1,0:T(4,128)S(1)}, s32[4]{0:T(128)}, s32[]{:T(128)}, /*index=5*/bf16[4,640,3,64]{1,3,2,0:T...) while((s32[]{:T(128)}, f32[3,640]{1,0:T(4,128)S(1)}, f32[3,640]{1,0:T(4,128)S(1)}, ...), condition=%wide.region_3.4_spmd.clone, body=%wide.region_0.3_spmd.clone.sunk | while | flops 165898880 | bytes 10424316 | solution.py:95
  93.4 4.1 %bitcast_reduce_fusion.2 = (f32[3,640]{1,0:T(4,128)S(1)}, f32[3,640,640]{2,1,0:T(8,128)}) fusion(pred[640]{0:T(1024)(128)(4,1)S(1)} %add_compare_fusion.7, bf16[640,3,64]{0,2,1:T(8,128)(2,1)S(1)} %get-tuple-element.670, bf16[4,640,3,64]{1,3,2,0:T(8,128)(2,1)} %get-tuple-element.669, s32[]{:T(128)} %get-tuple-element.655), kind=kOutput, calls=%fused_computation.1.clone.1 | convolution fusion | flops 160970880 | bytes 5415552 | tf_op jit(solution)/shard_map/while/body/eval_jaxpr/thd,khd->htk/dot_general | solution.py:75
  97.5 3.4 fusion.146
  103.6 4.1 %bitcast_reduce_fusion.2 = (f32[3,640]{1,0:T(4,128)S(1)}, f32[3,640,640]{2,1,0:T(8,128)}) fusion(pred[640]{0:T(1024)(128)(4,1)S(1)} %add_compare_fusion.7, bf16[640,3,64]{0,2,1:T(8,128)(2,1)S(1)} %get-tuple-element.670, bf16[4,640,3,64]{1,3,2,0:T(8,128)(2,1)} %get-tuple-element.669, s32[]{:T(128)} %get-tuple-element.655), kind=kOutput, calls=%fused_computation.1.clone.1 | convolution fusion | flops 160970880 | bytes 5415552 | tf_op jit(solution)/shard_map/while/body/eval_jaxpr/thd,khd->htk/dot_general | solution.py:75
  107.8 3.4 fusion.146
  113.9 4.1 %bitcast_reduce_fusion.2 = (f32[3,640]{1,0:T(4,128)S(1)}, f32[3,640,640]{2,1,0:T(8,128)}) fusion(pred[640]{0:T(1024)(128)(4,1)S(1)} %add_compare_fusion.7, bf16[640,3,64]{0,2,1:T(8,128)(2,1)S(1)} %get-tuple-element.670, bf16[4,640,3,64]{1,3,2,0:T(8,128)(2,1)} %get-tuple-element.669, s32[]{:T(128)} %get-tuple-element.655), kind=kOutput, calls=%fused_computation.1.clone.1 | convolution fusion | flops 160970880 | bytes 5415552 | tf_op jit(solution)/shard_map/while/body/eval_jaxpr/thd,khd->htk/dot_general | solution.py:75
  118.1 3.4 fusion.146
  124.2 4.1 %bitcast_reduce_fusion.2 = (f32[3,640]{1,0:T(4,128)S(1)}, f32[3,640,640]{2,1,0:T(8,128)}) fusion(pred[640]{0:T(1024)(128)(4,1)S(1)} %add_compare_fusion.7, bf16[640,3,64]{0,2,1:T(8,128)(2,1)S(1)} %get-tuple-element.670, bf16[4,640,3,64]{1,3,2,0:T(8,128)(2,1)} %get-tuple-element.669, s32[]{:T(128)} %get-tuple-element.655), kind=kOutput, calls=%fused_computation.1.clone.1 | convolution fusion | flops 160970880 | bytes 5415552 | tf_op jit(solution)/shard_map/while/body/eval_jaxpr/thd,khd->htk/dot_general | solution.py:75
  128.4 3.4 fusion.146
  133.8 22.0 %while.38 = (s32[]{:T(128)}, f32[640,3,64]{0,2,1:T(8,128)S(1)}, bf16[4,640,3,64]{1,3,2,0:T(8,128)(2,1)}, s32[4]{0:T(128)}, s32[]{:T(128)}, /*index=5*/bf16[4,640...) while((s32[]{:T(128)}, f32[640,3,64]{0,2,1:T(8,128)S(1)}, ...), condition=%wide.region_5.6_spmd.clone, body=%wide.region_4.5_spmd.clone.sunk | while | flops 319735040 | bytes 1730435 | solution.py:111
  142.0 2.8 fusion.151
  153.0 2.8 fusion.151
  156.5 14.1 %collective-permute-start = (bf16[31,192]{1,0:T(8,128)(2,1)S(1)}, bf16[31,192]{1,0:T(8,128)(2,1)S(1)}, u32[]{:S(2)}, u32[]{:S(2)}) collective-permute-start(bf16[31,192]{1,0:T(8,128)(2,1)S(1)} %slice.531), channel_id=1, source_target_pairs={{0,4},{4,8},{8,12},{1,5},{5,9},{9,13},{2,6},{6,10},{10,14},{3,7},{... | collective-permute-start | bytes 35720 | tf_op jit(solution)/shard_map/ppermute | solution.py:29
  172.2 7.1 %fusion.71 = (f32[192]{0:T(256)S(1)}, f32[192]{0:T(256)S(1)}, f32[192]{0:T(256)S(1)}, f32[192]{0:T(256)S(1)}, f32[192]{0:T(256)}, /*index=5*/f32[192]{0:T(256)},...) fusion(f32[671,192]{1,0:T(8,128)S(1)} %maximum_convert_fusion, ...), kind=kLoop, calls=%fused_computation.113 | loop fusion | flops 13636224 | bytes 16750720 | tf_op jit(solution)/shard_map/reduce_sum | solution.py:139
  180.6 5.5 %collective-permute-done.1 = bf16[31,192]{1,0:T(8,128)(2,1)S(1)} collective-permute-done((bf16[31,192]{1,0:T(8,128)(2,1)S(1)}, bf16[31,192]{1,0:T(8,128)(2,1)S(1)}, u32[]{:S(2)}, u32[]{:S(2)}) %collective-permute-start.1) | collective-permute-done | bytes 11936 | tf_op jit(solution)/shard_map/ppermute | solution.py:29
  186.2 3.1 fusion.75
  191.2 69.7 %while.39 = (s32[]{:T(128)}, f32[640,3,64]{0,2,1:T(8,128)}, bf16[4,640,384]{2,1,0:T(8,128)(2,1)}, bf16[4,640,3,64]{1,3,2,0:T(8,128)(2,1)}, s32[4]{0:T(128)}, /*i...) while((s32[]{:T(128)}, f32[640,3,64]{0,2,1:T(8,128)}, ...), condition=%wide.region_8.9_spmd.clone, body=%wide.region_7.8_spmd.clone.sunk | while | flops 800195840 | bytes 28289564 | solution.py:184
  261.0 2.9 fusion.70
  264.5 44.8 %reduce-scatter.2.cloned.1.call-done = bf16[640,384]{1,0:T(8,128)(2,1)} async-done(((bf16[2560,384]{1,0:T(8,128)(2,1)}), bf16[640,384]{1,0:T(8,128)(2,1)}) %reduce-scatter.2.cloned.1.call-update) | async-done | bytes 491536 | tf_op jit(solution)/shard_map/reduce_scatter | solution.py:189
  312.1 3.6 all-to-all-start.2
  318.8 19.1 %collective-permute-done.2 = f32[32,768]{1,0:T(8,128)S(1)} collective-permute-done((f32[32,768]{1,0:T(8,128)S(1)}, f32[32,768]{1,0:T(8,128)S(1)}, u32[]{:S(2)}, u32[]{:S(2)}) %collective-permute-start.2) | collective-permute-done | bytes 98336 | tf_op jit(solution)/shard_map/ppermute | solution.py:37
  339.9 3.2 collective-permute-done.3
  345.5 4.4 %collective-permute-done.4 = f32[32,768]{1,0:T(8,128)S(1)} collective-permute-done((f32[32,768]{1,0:T(8,128)S(1)}, f32[32,768]{1,0:T(8,128)S(1)}, u32[]{:S(2)}, u32[]{:S(2)}) %collective-permute-start.4) | collective-permute-done | bytes 98336 | tf_op jit(solution)/shard_map/ppermute | solution.py:37
  352.5 7.1 %collective-permute-done.5 = f32[32,768]{1,0:T(8,128)S(1)} collective-permute-done((f32[32,768]{1,0:T(8,128)S(1)}, f32[32,768]{1,0:T(8,128)S(1)}, u32[]{:S(2)}, u32[]{:S(2)}) %collective-permute-start.5) | collective-permute-done | bytes 98336 | tf_op jit(solution)/shard_map/ppermute | solution.py:37
  361.0 3.0 collective-permute-start.7
  364.0 3.4 collective-permute-done.7
  367.9 4.2 %collective-permute-done.8 = f32[32,768]{1,0:T(8,128)S(1)} collective-permute-done((f32[32,768]{1,0:T(8,128)S(1)}, f32[32,768]{1,0:T(8,128)S(1)}, u32[]{:S(2)}, u32[]{:S(2)}) %collective-permute-start.8) | collective-permute-done | bytes 98336 | tf_op jit(solution)/shard_map/ppermute | solution.py:37
  374.3 4.1 %collective-permute-done.9 = f32[32,768]{1,0:T(8,128)S(1)} collective-permute-done((f32[32,768]{1,0:T(8,128)S(1)}, f32[32,768]{1,0:T(8,128)S(1)}, u32[]{:S(2)}, u32[]{:S(2)}) %collective-permute-start.9) | collective-permute-done | bytes 98336 | tf_op jit(solution)/shard_map/ppermute | solution.py:37
  (246 shorter events, 143.2 us)
Async XLA Ops:
  40.1 43.3 %all-to-all-start.1 = ((bf16[4,640,384]{1,2,0:T(8,128)(2,1)}), bf16[4,640,384]{1,2,0:T(8,128)(2,1)}, u32[]{:S(2)}, u32[]{:S(2)}) async-start(bf16[4,640,384]{1,2,0:T(8,128)(2,1)} %stack.146), calls=%async_computation.1 | async-start | bytes 3932160 | tf_op jit(solution)/shard_map/all_to_all | solution.py:15
  47.6 261.7 %reduce-scatter.2.cloned.1.call-start = ((), (), s32[]{:S(2)}) async-start(), calls=%async_computation.4 | async-start | bytes 2457600 | tf_op jit(solution)/shard_map/reduce_scatter | solution.py:189
  133.8 22.5 %copy-start.3 = (bf16[1,4,160,1,192]{4,2,0,1,3:T(8,128)(2,1)S(1)}, bf16[1,4,160,1,192]{4,2,0,1,3:T(8,128)(2,1)}, u32[]{:S(2)}) copy-start(bf16[1,4,160,1,192]{4,2,0,1,3:T(8,128)(2,1)} %get-tuple-element.447) | copy-start | bytes 737284
  155.9 16.2 %copy-start.6 = (bf16[1,4,160,1,192]{4,2,0,1,3:T(8,128)(2,1)S(1)}, bf16[1,4,160,1,192]{4,2,0,1,3:T(8,128)(2,1)}, u32[]{:S(2)}) copy-start(bf16[1,4,160,1,192]{4,2,0,1,3:T(8,128)(2,1)} %get-tuple-element.443) | copy-start | bytes 737284
  155.9 16.2 %copy-start.11 = (f32[1,192]{1,0:T(1,128)S(1)}, f32[1,192]{1,0:T(1,128)}, u32[]{:S(2)}) copy-start(f32[1,192]{1,0:T(1,128)} %get-tuple-element.451) | copy-start | bytes 2308
  155.9 16.2 %copy-start.12 = (f32[1,192]{1,0:T(1,128)S(1)}, f32[1,192]{1,0:T(1,128)}, u32[]{:S(2)}) copy-start(f32[1,192]{1,0:T(1,128)} %get-tuple-element.452) | copy-start | bytes 2308
  155.9 16.2 %copy-start.13 = (f32[1,192]{1,0:T(1,128)S(1)}, f32[1,192]{1,0:T(1,128)}, u32[]{:S(2)}) copy-start(f32[1,192]{1,0:T(1,128)} %get-tuple-element.453) | copy-start | bytes 2308
  155.9 16.1 %copy-start.14 = (f32[1,192]{1,0:T(1,128)S(1)}, f32[1,192]{1,0:T(1,128)}, u32[]{:S(2)}) copy-start(f32[1,192]{1,0:T(1,128)} %get-tuple-element.454) | copy-start | bytes 2308
  155.9 16.1 %copy-start.15 = (f32[1,192]{1,0:T(1,128)S(1)}, f32[1,192]{1,0:T(1,128)}, u32[]{:S(2)}) copy-start(f32[1,192]{1,0:T(1,128)} %get-tuple-element.455) | copy-start | bytes 2308
  155.9 16.1 %copy-start.16 = (f32[1,192]{1,0:T(1,128)S(1)}, f32[1,192]{1,0:T(1,128)}, u32[]{:S(2)}) copy-start(f32[1,192]{1,0:T(1,128)} %get-tuple-element.456) | copy-start | bytes 2308
  155.9 16.1 %copy-start.17 = (f32[1,192]{1,0:T(1,128)S(1)}, f32[1,192]{1,0:T(1,128)}, u32[]{:S(2)}) copy-start(f32[1,192]{1,0:T(1,128)} %get-tuple-element.457) | copy-start | bytes 2308
  155.9 16.1 %copy-start.18 = (f32[1,192]{1,0:T(1,128)S(1)}, f32[1,192]{1,0:T(1,128)}, u32[]{:S(2)}) copy-start(f32[1,192]{1,0:T(1,128)} %get-tuple-element.458) | copy-start | bytes 2308
  156.0 16.1 %copy-start.19 = (f32[1,192]{1,0:T(1,128)S(1)}, f32[1,192]{1,0:T(1,128)}, u32[]{:S(2)}) copy-start(f32[1,192]{1,0:T(1,128)} %get-tuple-element.459) | copy-start | bytes 2308
  156.0 16.1 %copy-start.20 = (f32[1,192]{1,0:T(1,128)S(1)}, f32[1,192]{1,0:T(1,128)}, u32[]{:S(2)}) copy-start(f32[1,192]{1,0:T(1,128)} %get-tuple-element.460) | copy-start | bytes 2308
  156.0 16.1 %copy-start.21 = (f32[1,192]{1,0:T(1,128)S(1)}, f32[1,192]{1,0:T(1,128)}, u32[]{:S(2)}) copy-start(f32[1,192]{1,0:T(1,128)} %get-tuple-element.461) | copy-start | bytes 2308
  156.0 16.1 %copy-start.22 = (f32[1,192]{1,0:T(1,128)S(1)}, f32[1,192]{1,0:T(1,128)}, u32[]{:S(2)}) copy-start(f32[1,192]{1,0:T(1,128)} %get-tuple-element.462) | copy-start | bytes 2308
  156.0 16.1 %copy-start.23 = (f32[1,192]{1,0:T(1,128)S(1)}, f32[1,192]{1,0:T(1,128)}, u32[]{:S(2)}) copy-start(f32[1,192]{1,0:T(1,128)} %get-tuple-element.463) | copy-start | bytes 2308
  156.0 16.1 %copy-start.24 = (f32[1,192]{1,0:T(1,128)S(1)}, f32[1,192]{1,0:T(1,128)}, u32[]{:S(2)}) copy-start(f32[1,192]{1,0:T(1,128)} %get-tuple-element.464) | copy-start | bytes 2308
  156.0 16.1 %copy-start.25 = (f32[1,192]{1,0:T(1,128)S(1)}, f32[1,192]{1,0:T(1,128)}, u32[]{:S(2)}) copy-start(f32[1,192]{1,0:T(1,128)} %get-tuple-element.465) | copy-start | bytes 2308
  156.0 16.1 %copy-start.26 = (f32[1,192]{1,0:T(1,128)S(1)}, f32[1,192]{1,0:T(1,128)}, u32[]{:S(2)}) copy-start(f32[1,192]{1,0:T(1,128)} %get-tuple-element.466) | copy-start | bytes 2308
  156.5 15.4 %collective-permute-start = (bf16[31,192]{1,0:T(8,128)(2,1)S(1)}, bf16[31,192]{1,0:T(8,128)(2,1)S(1)}, u32[]{:S(2)}, u32[]{:S(2)}) collective-permute-start(bf16[31,192]{1,0:T(8,128)(2,1)S(1)} %slice.531), channel_id=1, source_target_pairs={{0,4},{4,8},{8,12},{1,5},{5,9},{9,13},{2,6},{6,10},{10,14},{3,7},{... | collective-permute-start | bytes 35720 | tf_op jit(solution)/shard_map/ppermute | solution.py:29
  179.3 6.8 %collective-permute-start.1 = (bf16[31,192]{1,0:T(8,128)(2,1)S(1)}, bf16[31,192]{1,0:T(8,128)(2,1)S(1)}, u32[]{:S(2)}, u32[]{:S(2)}) collective-permute-start(bf16[31,192]{1,0:T(8,128)(2,1)S(1)} %slice.596), channel_id=1, source_target_pairs={{4,0},{8,4},{12,8},{5,1},{9,5},{13,9},{6,2},{10,6},{14,10},{7,3},{... | collective-permute-start | bytes 35720 | tf_op jit(solution)/shard_map/ppermute | solution.py:29
  263.9 46.7 %copy-start.5 = (bf16[640,192]{1,0:T(8,128)(2,1)S(1)}, bf16[640,192]{1,0:T(8,128)(2,1)}, u32[]{:S(2)}) copy-start(bf16[640,192]{1,0:T(8,128)(2,1)} %copy-done.4) | copy-start | bytes 737284
  312.1 67.0 %all-to-all-start.2 = ((bf16[5,4,160,1,192]{4,2,3,0,1:T(8,128)(2,1)}), bf16[5,4,160,1,192]{4,2,3,0,1:T(8,128)(2,1)S(1)}, u32[]{:S(2)}, u32[]{:S(2)}) async-start(bf16[5,4,160,1,192]{4,2,3,0,1:T(8,128)(2,1)} %copy.93), calls=%async_computation.3 | async-start | bytes 3276800 | tf_op jit(solution)/shard_map/all_to_all | solution.py:204
  316.4 21.5 %collective-permute-start.2 = (f32[32,768]{1,0:T(8,128)S(1)}, f32[32,768]{1,0:T(8,128)S(1)}, u32[]{:S(2)}, u32[]{:S(2)}) collective-permute-start(f32[32,768]{1,0:T(8,128)S(1)} %dynamic_update_slice.9), channel_id=1, source_target_pairs={{0,1},{1,0},{2,3},{3,2},{4,5},{5,4},{6,7},{7,6},{8,9},{9,8},{10,11... | collective-permute-start | bytes 294920 | tf_op jit(solution)/shard_map/ppermute | solution.py:37
  338.4 4.7 %collective-permute-start.3 = (f32[32,768]{1,0:T(8,128)S(1)}, f32[32,768]{1,0:T(8,128)S(1)}, u32[]{:S(2)}, u32[]{:S(2)}) collective-permute-start(f32[32,768]{1,0:T(8,128)S(1)} %add.364), channel_id=1, source_target_pairs={{0,2},{1,3},{2,0},{3,1},{4,6},{5,7},{6,4},{7,5},{8,10},{9,11},{10,... | collective-permute-start | bytes 294920 | tf_op jit(solution)/shard_map/ppermute | solution.py:37
  343.1 6.8 %collective-permute-start.4 = (f32[32,768]{1,0:T(8,128)S(1)}, f32[32,768]{1,0:T(8,128)S(1)}, u32[]{:S(2)}, u32[]{:S(2)}) collective-permute-start(f32[32,768]{1,0:T(8,128)S(1)} %add.365), channel_id=1, source_target_pairs={{0,4},{4,0},{8,12},{12,8},{1,5},{5,1},{9,13},{13,9},{2,6},{6,2},{1... | collective-permute-start | bytes 294920 | tf_op jit(solution)/shard_map/ppermute | solution.py:37
  349.9 9.6 %collective-permute-start.5 = (f32[32,768]{1,0:T(8,128)S(1)}, f32[32,768]{1,0:T(8,128)S(1)}, u32[]{:S(2)}, u32[]{:S(2)}) collective-permute-start(f32[32,768]{1,0:T(8,128)S(1)} %add.366), channel_id=1, source_target_pairs={{0,8},{4,12},{8,0},{12,4},{1,9},{5,13},{9,1},{13,5},{2,10},{6,14},... | collective-permute-start | bytes 294920 | tf_op jit(solution)/shard_map/ppermute | solution.py:37
  359.6 1.4 collective-permute-start.6
  361.0 6.4 %collective-permute-start.7 = (f32[32,768]{1,0:T(8,128)S(1)}, f32[32,768]{1,0:T(8,128)S(1)}, u32[]{:S(2)}, u32[]{:S(2)}) collective-permute-start(f32[32,768]{1,0:T(8,128)S(1)} %add.368), channel_id=1, source_target_pairs={{0,32},{16,48},{32,0},{48,16},{64,96},{80,112},{96,64},{112,80},{1... | collective-permute-start | bytes 294920 | tf_op jit(solution)/shard_map/ppermute | solution.py:37
  367.4 4.7 %collective-permute-start.8 = (f32[32,768]{1,0:T(8,128)S(1)}, f32[32,768]{1,0:T(8,128)S(1)}, u32[]{:S(2)}, u32[]{:S(2)}) collective-permute-start(f32[32,768]{1,0:T(8,128)S(1)} %add.369), channel_id=1, source_target_pairs={{0,64},{16,80},{32,96},{48,112},{64,0},{80,16},{96,32},{112,48},{1... | collective-permute-start | bytes 294920 | tf_op jit(solution)/shard_map/ppermute | solution.py:37
  372.2 6.2 %collective-permute-start.9 = (f32[32,768]{1,0:T(8,128)S(1)}, f32[32,768]{1,0:T(8,128)S(1)}, u32[]{:S(2)}, u32[]{:S(2)}) collective-permute-start(f32[32,768]{1,0:T(8,128)S(1)} %add.370), channel_id=1, source_target_pairs={{0,128},{16,144},{32,160},{48,176},{64,192},{80,208},{96,224},{112... | collective-permute-start | bytes 294920 | tf_op jit(solution)/shard_map/ppermute | solution.py:37
  (24 other events, 125.3 us)
Sparse Core Ops, SparseCore 0:
  261.1 48.1 reduce-scatter.1
